TPU v7x, 32 devices: a whole 2x2x4 slice. The times are simulated.
32 devices in a mesh: grp: 2 (over y), cell: 8 (over z, x), gene: 2 (over core).
Axes of the slice: x: 2, y: 2, z: 4, core: 2. Of those that a mesh axis runs over, the one named last changes fastest.
Arguments:
- expression: bfloat16 [2048, 16384], P(('grp', 'cell'), 'gene'), parts along dimension 0, may hold values from -6 to 6
- design: bfloat16 [2048, 128], P(('grp', 'cell')), parts along dimension 0, may hold values from -24 to 24
- quantile_level: float32 [16384], P('gene'), may hold values from 0.1 to 0.9
Outputs:
- quantile_slack: bfloat16 [2048, 16384], P(('grp', 'cell'), 'gene'), parts along dimension 0
- low_rank_coef: float32 [32768, 128], P(('grp', 'gene', 'cell')), parts along dimension 0
There are 2 independent parts, one for each index of `grp`. A program takes and returns all parts, laid end to end along the dimension named above; an argument that names none is the same for every part. Nothing has to cross between parts.
All inputs are finite; a program needn't handle non-finite values.
Results may differ from a plain program's by a relative error of at most 0.0025.
The roundings to bfloat16 on the way count: a program that leaves them out, or rounds other values in their place, can miss the bound.
Values may be sent and summed in bfloat16 or wider, within the bound.
No kernel may reach another device: no remote copies, remote signals or barrier semaphores. Data moves between devices by JAX's collectives and lax.ppermute only.
A program may use at most 64 MiB of HBM per device.

v0:
```python
import functools
import math
import jax
import jax.numpy as jnp
from jax import lax
from jax.sharding import PartitionSpec as P

NS_STEPS = 8
shrink_rate = 0.25


def matmul(left, right):
    return jnp.dot(left, right, precision=lax.Precision.HIGHEST)


def invert(matrix):
    identity = jnp.eye(matrix.shape[0], dtype=jnp.float32)
    factor = jnp.linalg.cholesky(matrix)
    lower_inv = lax.linalg.triangular_solve(factor, identity, left_side=True, lower=True)
    return matmul(lower_inv.T, lower_inv)


def newton(moment):
    identity = jnp.eye(moment.shape[0], dtype=jnp.float32)
    current = moment / jnp.trace(moment)
    root_inv = identity
    for sweep in range(NS_STEPS):
        middle = 1.5 * identity - 0.5 * matmul(root_inv, current)
        current = matmul(current, middle)
        root_inv = matmul(middle, root_inv)
    return root_inv


def cell_ring(mesh):
    devices = mesh.devices
    names = list(mesh.axis_names)
    index = [0] * len(names)
    index[names.index("cell")] = slice(None)
    line = list(devices[tuple(index)].reshape(-1))
    n = len(line)
    try:
        coords = [tuple(d.coords) for d in line]
    except (AttributeError, TypeError):
        return list(range(n))
    varying = [a for a in range(len(coords[0])) if len({c[a] for c in coords}) > 1]
    where = {c: i for i, c in enumerate(coords)}
    if len(varying) == 1:
        return sorted(range(n), key=lambda i: coords[i][varying[0]])
    if len(varying) != 2:
        return list(range(n))
    sizes = [len({c[a] for c in coords}) for a in varying]
    if sizes[0] * sizes[1] != n:
        return list(range(n))
    if sizes[0] % 2:
        varying, sizes = (varying[::-1], sizes[::-1])
        if sizes[0] % 2:
            return list(range(n))
    lows = [min((c[a] for c in coords)) for a in varying]
    path = []
    for u in range(sizes[0]):
        span = range(1, sizes[1]) if u % 2 == 0 else range(sizes[1] - 1, 0, -1)
        path += [(u, v) for v in span]
    path += [(u, 0) for u in range(sizes[0] - 1, -1, -1)]
    order = []
    for u, v in path:
        key = list(coords[0])
        key[varying[0]] = lows[0] + u
        key[varying[1]] = lows[1] + v
        order.append(where[tuple(key)])
    return order


def gather_blocks(block, axis):
    n = lax.axis_size(axis)
    me = lax.axis_index(axis)
    received = [block]
    for shift in range(1, n):
        pairs = [(i, (i + shift) % n) for i in range(n)]
        received.append(lax.ppermute(block, axis, pairs))
    stacked = jnp.stack(received)
    return jnp.take(stacked, (me - jnp.arange(n)) % n, axis=0)


def butterfly_sum(value, axis):
    n = lax.axis_size(axis)
    if n & n - 1:
        return lax.psum(value, axis)
    bit = 1
    while bit < n:
        pairs = [(i, i ^ bit) for i in range(n)]
        value = value + lax.ppermute(value, axis, pairs)
        bit *= 2
    return value


def per_device(ring, expression, design, quantile_level):
    n = len(ring)
    width = design.shape[1]
    span = expression.shape[1] // n
    identity = jnp.eye(width, dtype=jnp.float32)
    design_all = gather_blocks(design, "cell").reshape(-1, width)
    sent = expression + (design_all[0, 0] * 0).astype(expression.dtype)
    expression_genes = lax.all_to_all(sent, "cell", 1, 0, tiled=True)
    gram_total = lax.dot_general(
        design_all, design_all, (((0,), (0,)), ((), ())), preferred_element_type=jnp.float32
    )
    inverse = invert(gram_total + identity)
    crossed = lax.dot_general(
        expression_genes, design_all, (((0,), (0,)), ((), ())), preferred_element_type=jnp.float32
    )
    coef = matmul(crossed, inverse)
    local_moment = lax.dot_general(
        coef, coef, (((0,), (0,)), ((), ())), precision=lax.Precision.HIGHEST
    )
    chip_moment = butterfly_sum(local_moment, "gene")
    moment = jnp.sum(gather_blocks(chip_moment, "cell"), axis=0)
    root_inv = newton(moment)
    low_rank_coef = coef - shrink_rate / math.sqrt(width) * matmul(coef, root_inv)
    coef_low_t = coef.astype(jnp.bfloat16).T
    ring_arr = jnp.array(ring, dtype=jnp.int32)
    pos_arr = jnp.array([ring.index(i) for i in range(n)], dtype=jnp.int32)
    me = lax.axis_index("cell")
    pos = pos_arr[me]
    forward = [(ring[q], ring[(q + 1) % n]) for q in range(n)]
    backward = [(ring[(q + 1) % n], ring[q]) for q in range(n)]
    out = jnp.zeros(expression.shape, jnp.bfloat16)

    def place(out, block, owner):
        start = owner * span
        fitted = jnp.dot(design, block, preferred_element_type=jnp.float32)
        local = lax.dynamic_slice_in_dim(expression, start, span, axis=1).astype(jnp.float32)
        level = lax.dynamic_slice_in_dim(quantile_level, start, span)[None, :]
        slack = local - fitted
        piece = (slack - jnp.clip(slack, level - 1.0, level)).astype(jnp.bfloat16)
        return lax.dynamic_update_slice_in_dim(out, piece, start, axis=1)

    out = place(out, coef_low_t, me)
    ahead, behind = (coef_low_t, coef_low_t)
    for step in range(1, n // 2 + 1):
        ahead = lax.ppermute(ahead, "cell", forward)
        out = place(out, ahead, ring_arr[(pos - step) % n])
        if step <= (n - 1) // 2:
            behind = lax.ppermute(behind, "cell", backward)
            out = place(out, behind, ring_arr[(pos + step) % n])
    return (out, low_rank_coef)


def solution(mesh):
    placed = (P(("grp", "cell"), "gene"), P(("grp", "cell"), None), P("gene"))
    ring = cell_ring(mesh)
    return jax.shard_map(
        functools.partial(per_device, ring),
        mesh=mesh,
        in_specs=placed,
        out_specs=(P(("grp", "cell"), "gene"), P(("grp", "gene", "cell"), None)),
        check_vma=False,
    )
```

profile of v0, /device:TPU:0, one launch (start us, length us, event | category | flops | bytes accessed | tf_op | source)
XLA Modules:
  0.0 163.7 jit_solution(11076976861056799472)
XLA Ops:
  0.6 6.1 %collective-permute-start.6 = (bf16[128,128]{1,0:T(8,128)(2,1)}, bf16[128,128]{1,0:T(8,128)(2,1)S(1)}, u32[]{:S(2)}, u32[]{:S(2)}) collective-permute-start(bf16[128,128]{1,0:T(8,128)(2,1)} %param.6), channel_id=1, source_target_pairs={{0,14},{2,0},{4,2},{6,4},{8,6},{10,8},{12,10},{14,12},{1,15},{3,1}... | collective-permute-start | bytes 98312 | tf_op jit(solution)/shard_map/ppermute | solution.py:79
  7.1 3.0 %collective-permute-start.3 = (bf16[128,128]{1,0:T(8,128)(2,1)}, bf16[128,128]{1,0:T(8,128)(2,1)S(1)}, u32[]{:S(2)}, u32[]{:S(2)}) collective-permute-start(bf16[128,128]{1,0:T(8,128)(2,1)} %param.6), channel_id=1, source_target_pairs={{0,8},{2,10},{4,12},{6,14},{8,0},{10,2},{12,4},{14,6},{1,9},{3,11}... | collective-permute-start | bytes 98312 | tf_op jit(solution)/shard_map/ppermute | solution.py:79
  10.1 1.5 collective-permute-start
  11.7 0.8 constant_dynamic-update-slice_fusion.7
  13.1 3.2 %copy.43 = bf16[128,8192]{0,1:T(8,128)(2,1)S(1)} copy(bf16[128,8192]{1,0:T(8,128)(2,1)} %param.5) | data formatting | bytes 4194304 | tf_op args[0]
  16.3 0.7 collective-permute-done
  17.0 5.7 %collective-permute-done.1 = bf16[128,128]{1,0:T(8,128)(2,1)S(1)} collective-permute-done((bf16[128,128]{1,0:T(8,128)(2,1)S(1)}, bf16[128,128]{1,0:T(8,128)(2,1)S(1)}, u32[]{:S(2)}, u32[]{:S(2)}) %collective-permute-start.1) | collective-permute-done | bytes 32800 | tf_op jit(solution)/shard_map/ppermute | solution.py:79
  22.7 5.7 %collective-permute-done.2 = bf16[128,128]{1,0:T(8,128)(2,1)S(1)} collective-permute-done((bf16[128,128]{1,0:T(8,128)(2,1)S(1)}, bf16[128,128]{1,0:T(8,128)(2,1)S(1)}, u32[]{:S(2)}, u32[]{:S(2)}) %collective-permute-start.2) | collective-permute-done | bytes 32800 | tf_op jit(solution)/shard_map/ppermute | solution.py:79
  30.9 1.5 broadcast_add_fusion
  32.4 3.9 %copy.45 = bf16[128,8,1024]{2,0,1:T(8,128)(2,1)} copy(bf16[128,8,1024]{0,2,1:T(8,128)(2,1)} %bitcast.190) | data formatting | bytes 4194304 | tf_op jit(solution)/shard_map/all_to_all | solution.py:103
  36.3 4.5 %all-to-all-start = ((bf16[128,8,1024]{2,0,1:T(8,128)(2,1)}), bf16[128,8,1024]{2,0,1:T(8,128)(2,1)}, u32[]{:S(2)}, u32[]{:S(2)}) async-start(bf16[128,8,1024]{2,0,1:T(8,128)(2,1)} %copy.45), calls=%async_computation | async-start | bytes 4194304 | tf_op jit(solution)/shard_map/all_to_all | solution.py:103
  46.1 0.7 fusion.35
  51.3 0.6 broadcast_add_fusion.1
  52.4 11.7 %cholesky.29 = f32[128,128]{1,0:T(8,128)S(1)} custom-call(f32[128,128]{1,0:T(8,128)S(1)} %fusion.27), custom_call_target="Cholesky" | custom-call | tf_op jit(solution)/shard_map/jit(cholesky)/cholesky | solution.py:18
  64.2 0.6 compare_reduce_fusion
  64.8 0.7 fusion.23
  65.5 9.8 %custom-call.6 = f32[1,128,128]{1,2,0:T(8,128)S(1)} custom-call(f32[1,128,128]{2,1,0:T(8,128)S(1)} %fusion.23), custom_call_target="InvertDiagBlocksLowerTriangular" | custom-call | tf_op jit(solution)/shard_map/triangular_solve | solution.py:19
  75.8 9.4 %all-to-all-done = bf16[128,8,1024]{2,0,1:T(8,128)(2,1)} async-done(((bf16[128,8,1024]{2,0,1:T(8,128)(2,1)}), bf16[128,8,1024]{2,0,1:T(8,128)(2,1)}, u32[]{:S(2)}, u32[]{:S(2)}) %all-to-all-start) | async-done | bytes 2097184 | tf_op jit(solution)/shard_map/all_to_all | solution.py:103
  85.2 3.9 %copy.46 = bf16[128,8,1024]{0,2,1:T(8,128)(2,1)} copy(bf16[128,8,1024]{2,0,1:T(8,128)(2,1)} %all-to-all-done) | data formatting | bytes 4194304 | tf_op jit(solution)/shard_map/all_to_all | solution.py:103
  89.1 2.4 %fusion.2 = f32[1024,128]{1,0:T(8,128)S(1)} fusion(bf16[128,8,1024]{0,2,1:T(8,128)(2,1)} %copy.46, bf16[8,128,128]{2,1,0:T(8,128)(2,1)S(1)} %gather_fusion, pred[8]{0:T(512)(128)(4,1)S(1)} %compare_and_fusion), kind=kOutput, calls=%fused_computation.4 | convolution fusion | flops 268566528 | bytes 2883592 | tf_op jit(solution)/shard_map/dot_general | solution.py:108
  92.1 1.0 fusion.38
  93.1 1.3 collective-permute-start.8
  94.4 0.8 collective-permute-start.7
  95.7 0.9 collective-permute-done.14
  96.6 1.5 bitcast_dynamic-update-slice_fusion.7
  98.1 1.3 collective-permute-start.15
  99.3 1.5 broadcast_in_dim.41
  100.9 0.7 constant_dynamic-update-slice_fusion.15
  101.6 1.4 collective-permute-start.20
  103.6 1.4 collective-permute-done.15
  105.6 0.6 bitcast_dynamic-update-slice_fusion.6
  106.2 4.9 %collective-permute-done.16 = f32[128,128]{1,0:T(8,128)S(1)} collective-permute-done((f32[128,128]{1,0:T(8,128)S(1)}, f32[128,128]{1,0:T(8,128)S(1)}, u32[]{:S(2)}, u32[]{:S(2)}) %collective-permute-start.16) | collective-permute-done | bytes 65568 | tf_op jit(solution)/shard_map/ppermute | solution.py:79
  111.1 0.7 collective-permute-start.17
  111.8 0.6 bitcast_dynamic-update-slice_fusion.5
  112.4 4.8 %collective-permute-done.17 = f32[128,128]{1,0:T(8,128)S(1)} collective-permute-done((f32[128,128]{1,0:T(8,128)S(1)}, f32[128,128]{1,0:T(8,128)S(1)}, u32[]{:S(2)}, u32[]{:S(2)}) %collective-permute-start.17) | collective-permute-done | bytes 65568 | tf_op jit(solution)/shard_map/ppermute | solution.py:79
  117.2 1.2 collective-permute-start.18
  118.4 0.6 bitcast_dynamic-update-slice_fusion.4
  119.0 3.5 %collective-permute-done.18 = f32[128,128]{1,0:T(8,128)S(1)} collective-permute-done((f32[128,128]{1,0:T(8,128)S(1)}, f32[128,128]{1,0:T(8,128)S(1)}, u32[]{:S(2)}, u32[]{:S(2)}) %collective-permute-start.18) | collective-permute-done | bytes 65568 | tf_op jit(solution)/shard_map/ppermute | solution.py:79
  123.2 0.6 bitcast_dynamic-update-slice_fusion.2
  123.9 0.6 bitcast_dynamic-update-slice_fusion.1
  124.5 2.3 %collective-permute-done.21 = f32[128,128]{1,0:T(8,128)S(1)} collective-permute-done((f32[128,128]{1,0:T(8,128)S(1)}, f32[128,128]{1,0:T(8,128)S(1)}, u32[]{:S(2)}, u32[]{:S(2)}) %collective-permute-start.21) | collective-permute-done | bytes 65568 | tf_op jit(solution)/shard_map/ppermute | solution.py:79
  126.8 0.6 bitcast_dynamic-update-slice_fusion
  127.5 1.6 gather_fusion.1
  129.1 0.8 select_reduce_fusion
  130.5 0.8 fusion.21
  131.3 0.8 fusion.29
  136.6 1.4 fusion.13
  138.4 1.3 subtract_convert_fusion.6
  139.7 1.3 subtract_convert_fusion.5
  141.3 1.8 %collective-permute-start.10 = (bf16[128,1024]{0,1:T(8,128)(2,1)}, bf16[128,1024]{0,1:T(8,128)(2,1)S(1)}, u32[]{:S(2)}, u32[]{:S(2)}) collective-permute-start(bf16[128,1024]{0,1:T(8,128)(2,1)} %collective-permute-done.8), channel_id=1, source_target_pairs={{8,4},{12,8},{14,12},{10,14},{6,10},{2,6},{0,2},{4,0},{9,5},{13,9}... | collective-permute-start | bytes 786440 | tf_op jit(solution)/shard_map/ppermute | solution.py:143
  143.2 0.7 constant_dynamic-update-slice_fusion.14
  143.9 0.7 constant_dynamic-update-slice_fusion.13
  144.6 2.3 %collective-permute-done.9 = bf16[128,1024]{0,1:T(8,128)(2,1)S(1)} collective-permute-done((bf16[128,1024]{0,1:T(8,128)(2,1)}, bf16[128,1024]{0,1:T(8,128)(2,1)S(1)}, u32[]{:S(2)}, u32[]{:S(2)}) %collective-permute-start.9) | collective-permute-done | bytes 262176 | tf_op jit(solution)/shard_map/ppermute | solution.py:140
  147.5 1.5 collective-permute-done.10
  149.0 0.7 copy-done.7
  150.4 1.9 %collective-permute-start.12 = (bf16[128,1024]{0,1:T(8,128)(2,1)}, bf16[128,1024]{0,1:T(8,128)(2,1)S(1)}, u32[]{:S(2)}, u32[]{:S(2)}) collective-permute-start(bf16[128,1024]{0,1:T(8,128)(2,1)} %copy-done.7), channel_id=1, source_target_pairs={{8,4},{12,8},{14,12},{10,14},{6,10},{2,6},{0,2},{4,0},{9,5},{13,9}... | collective-permute-start | bytes 786440 | tf_op jit(solution)/shard_map/ppermute | solution.py:143
  152.3 0.7 constant_dynamic-update-slice_fusion.12
  153.0 0.7 constant_dynamic-update-slice_fusion.11
  153.7 2.4 %collective-permute-done.11 = bf16[128,1024]{0,1:T(8,128)(2,1)S(1)} collective-permute-done((bf16[128,1024]{0,1:T(8,128)(2,1)S(1)}, bf16[128,1024]{0,1:T(8,128)(2,1)S(1)}, u32[]{:S(2)}, u32[]{:S(2)}) %collective-permute-start.11) | collective-permute-done | bytes 262176 | tf_op jit(solution)/shard_map/ppermute | solution.py:140
  156.5 0.7 collective-permute-done.12
  157.8 0.7 constant_dynamic-update-slice_fusion.10
  158.6 0.7 constant_dynamic-update-slice_fusion.9
  159.3 3.2 %collective-permute-done.13 = bf16[128,1024]{0,1:T(8,128)(2,1)S(1)} collective-permute-done((bf16[128,1024]{0,1:T(8,128)(2,1)S(1)}, bf16[128,1024]{0,1:T(8,128)(2,1)S(1)}, u32[]{:S(2)}, u32[]{:S(2)}) %collective-permute-start.13) | collective-permute-done | bytes 262176 | tf_op jit(solution)/shard_map/ppermute | solution.py:140
  163.0 0.7 constant_dynamic-update-slice_fusion.8
  (96 shorter events, 15.1 us)
Async XLA Ops:
  0.6 27.9 %collective-permute-start.6 = (bf16[128,128]{1,0:T(8,128)(2,1)}, bf16[128,128]{1,0:T(8,128)(2,1)S(1)}, u32[]{:S(2)}, u32[]{:S(2)}) collective-permute-start(bf16[128,128]{1,0:T(8,128)(2,1)} %param.6), channel_id=1, source_target_pairs={{0,14},{2,0},{4,2},{6,4},{8,6},{10,8},{12,10},{14,12},{1,15},{3,1}... | collective-permute-start | bytes 98312 | tf_op jit(solution)/shard_map/ppermute | solution.py:79
  6.7 21.8 %collective-permute-start.5 = (bf16[128,128]{1,0:T(8,128)(2,1)}, bf16[128,128]{1,0:T(8,128)(2,1)S(1)}, u32[]{:S(2)}, u32[]{:S(2)}) collective-permute-start(bf16[128,128]{1,0:T(8,128)(2,1)} %param.6), channel_id=1, source_target_pairs={{0,12},{2,14},{4,0},{6,2},{8,4},{10,6},{12,8},{14,10},{1,13},{3,15... | collective-permute-start | bytes 98312 | tf_op jit(solution)/shard_map/ppermute | solution.py:79
  7.1 21.3 %collective-permute-start.4 = (bf16[128,128]{1,0:T(8,128)(2,1)}, bf16[128,128]{1,0:T(8,128)(2,1)S(1)}, u32[]{:S(2)}, u32[]{:S(2)}) collective-permute-start(bf16[128,128]{1,0:T(8,128)(2,1)} %param.6), channel_id=1, source_target_pairs={{0,10},{2,12},{4,14},{6,0},{8,2},{10,4},{12,6},{14,8},{1,11},{3,13... | collective-permute-start | bytes 98312 | tf_op jit(solution)/shard_map/ppermute | solution.py:79
  7.1 21.3 %collective-permute-start.3 = (bf16[128,128]{1,0:T(8,128)(2,1)}, bf16[128,128]{1,0:T(8,128)(2,1)S(1)}, u32[]{:S(2)}, u32[]{:S(2)}) collective-permute-start(bf16[128,128]{1,0:T(8,128)(2,1)} %param.6), channel_id=1, source_target_pairs={{0,8},{2,10},{4,12},{6,14},{8,0},{10,2},{12,4},{14,6},{1,9},{3,11}... | collective-permute-start | bytes 98312 | tf_op jit(solution)/shard_map/ppermute | solution.py:79
  10.1 6.8 %collective-permute-start = (bf16[128,128]{1,0:T(8,128)(2,1)}, bf16[128,128]{1,0:T(8,128)(2,1)S(1)}, u32[]{:S(2)}, u32[]{:S(2)}) collective-permute-start(bf16[128,128]{1,0:T(8,128)(2,1)} %param.6), channel_id=1, source_target_pairs={{0,2},{2,4},{4,6},{6,8},{8,10},{10,12},{12,14},{14,0},{1,3},{3,5},... | collective-permute-start | bytes 98312 | tf_op jit(solution)/shard_map/ppermute | solution.py:79
  11.7 77.5 %copy-start.6 = (pred[8]{0:T(512)(128)(4,1)}, pred[8]{0:T(512)(128)(4,1)S(1)}, u32[]{:S(2)}) copy-start(pred[8]{0:T(512)(128)(4,1)S(1)} %compare_and_fusion) | copy-start | bytes 28
  13.1 3.9 %copy-start = (bf16[128,128]{1,0:T(8,128)(2,1)S(1)}, bf16[128,128]{1,0:T(8,128)(2,1)}, u32[]{:S(2)}) copy-start(bf16[128,128]{1,0:T(8,128)(2,1)} %param.6) | copy-start | bytes 98308
  17.0 5.7 %collective-permute-start.1 = (bf16[128,128]{1,0:T(8,128)(2,1)S(1)}, bf16[128,128]{1,0:T(8,128)(2,1)S(1)}, u32[]{:S(2)}, u32[]{:S(2)}) collective-permute-start(bf16[128,128]{1,0:T(8,128)(2,1)S(1)} %copy-done), channel_id=1, source_target_pairs={{0,4},{2,6},{4,8},{6,10},{8,12},{10,14},{12,0},{14,2},{1,5},{3,7},... | collective-permute-start | bytes 98312 | tf_op jit(solution)/shard_map/ppermute | solution.py:79
  22.7 5.7 %collective-permute-start.2 = (bf16[128,128]{1,0:T(8,128)(2,1)S(1)}, bf16[128,128]{1,0:T(8,128)(2,1)S(1)}, u32[]{:S(2)}, u32[]{:S(2)}) collective-permute-start(bf16[128,128]{1,0:T(8,128)(2,1)S(1)} %copy-done), channel_id=1, source_target_pairs={{0,6},{2,8},{4,10},{6,12},{8,14},{10,0},{12,2},{14,4},{1,7},{3,9},... | collective-permute-start | bytes 98312 | tf_op jit(solution)/shard_map/ppermute | solution.py:79
  36.3 4.5 %copy-start.8 = (s32[8]{0:T(128)S(1)}, s32[8]{0:T(128)}, u32[]{:S(2)}) copy-start(s32[8]{0:T(128)} %constant.188.clone) | copy-start | bytes 100
  36.3 9.8 %copy-start.2 = (s32[8]{0:T(128)S(1)}, s32[8]{0:T(128)}, u32[]{:S(2)}) copy-start(s32[8]{0:T(128)} %constant.187.clone) | copy-start | bytes 100
  36.3 15.0 %copy-start.1 = (f32[8192]{0:T(1024)S(1)}, f32[8192]{0:T(1024)}, u32[]{:S(2)}) copy-start(f32[8192]{0:T(1024)} %param.7) | copy-start | bytes 98308
  36.3 48.9 %all-to-all-start = ((bf16[128,8,1024]{2,0,1:T(8,128)(2,1)}), bf16[128,8,1024]{2,0,1:T(8,128)(2,1)}, u32[]{:S(2)}, u32[]{:S(2)}) async-start(bf16[128,8,1024]{2,0,1:T(8,128)(2,1)} %copy.45), calls=%async_computation | async-start | bytes 4194304 | tf_op jit(solution)/shard_map/all_to_all | solution.py:103
  93.1 46.6 %collective-permute-start.8 = (bf16[128,1024]{0,1:T(8,128)(2,1)S(1)}, bf16[128,1024]{0,1:T(8,128)(2,1)}, u32[]{:S(2)}, u32[]{:S(2)}) collective-permute-start(bf16[128,1024]{0,1:T(8,128)(2,1)S(1)} %convert_bitcast_fusion), channel_id=1, source_target_pairs={{8,4},{12,8},{14,12},{10,14},{6,10},{2,6},{0,2},{4,0},{9,5},{13,9}... | collective-permute-start | bytes 786440 | tf_op jit(solution)/shard_map/ppermute | solution.py:143
  94.4 43.6 %collective-permute-start.7 = (bf16[128,1024]{0,1:T(8,128)(2,1)S(1)}, bf16[128,1024]{0,1:T(8,128)(2,1)}, u32[]{:S(2)}, u32[]{:S(2)}) collective-permute-start(bf16[128,1024]{0,1:T(8,128)(2,1)S(1)} %convert_bitcast_fusion), channel_id=1, source_target_pairs={{4,8},{8,12},{12,14},{14,10},{10,6},{6,2},{2,0},{0,4},{5,9},{9,13}... | collective-permute-start | bytes 786440 | tf_op jit(solution)/shard_map/ppermute | solution.py:140
  95.2 1.4 collective-permute-start.14
  98.1 7.0 %collective-permute-start.15 = (f32[128,128]{1,0:T(8,128)S(1)}, f32[128,128]{1,0:T(8,128)S(1)}, u32[]{:S(2)}, u32[]{:S(2)}) collective-permute-start(f32[128,128]{1,0:T(8,128)S(1)} %get-tuple-element.3), channel_id=1, source_target_pairs={{0,2},{2,4},{4,6},{6,8},{8,10},{10,12},{12,14},{14,0},{1,3},{3,5},... | collective-permute-start | bytes 196616 | tf_op jit(solution)/shard_map/ppermute | solution.py:79
  101.6 22.3 %collective-permute-start.20 = (f32[128,128]{1,0:T(8,128)S(1)}, f32[128,128]{1,0:T(8,128)S(1)}, u32[]{:S(2)}, u32[]{:S(2)}) collective-permute-start(f32[128,128]{1,0:T(8,128)S(1)} %get-tuple-element.3), channel_id=1, source_target_pairs={{0,12},{2,14},{4,0},{6,2},{8,4},{10,6},{12,8},{14,10},{1,13},{3,15... | collective-permute-start | bytes 196616 | tf_op jit(solution)/shard_map/ppermute | solution.py:79
  103.0 20.2 %collective-permute-start.19 = (f32[128,128]{1,0:T(8,128)S(1)}, f32[128,128]{1,0:T(8,128)S(1)}, u32[]{:S(2)}, u32[]{:S(2)}) collective-permute-start(f32[128,128]{1,0:T(8,128)S(1)} %get-tuple-element.3), channel_id=1, source_target_pairs={{0,10},{2,12},{4,14},{6,0},{8,2},{10,4},{12,6},{14,8},{1,11},{3,13... | collective-permute-start | bytes 196616 | tf_op jit(solution)/shard_map/ppermute | solution.py:79
  105.0 6.1 %collective-permute-start.16 = (f32[128,128]{1,0:T(8,128)S(1)}, f32[128,128]{1,0:T(8,128)S(1)}, u32[]{:S(2)}, u32[]{:S(2)}) collective-permute-start(f32[128,128]{1,0:T(8,128)S(1)} %get-tuple-element.3), channel_id=1, source_target_pairs={{0,4},{2,6},{4,8},{6,10},{8,12},{10,14},{12,0},{14,2},{1,5},{3,7},... | collective-permute-start | bytes 196616 | tf_op jit(solution)/shard_map/ppermute | solution.py:79
  111.1 6.1 %collective-permute-start.17 = (f32[128,128]{1,0:T(8,128)S(1)}, f32[128,128]{1,0:T(8,128)S(1)}, u32[]{:S(2)}, u32[]{:S(2)}) collective-permute-start(f32[128,128]{1,0:T(8,128)S(1)} %get-tuple-element.3), channel_id=1, source_target_pairs={{0,6},{2,8},{4,10},{6,12},{8,14},{10,0},{12,2},{14,4},{1,7},{3,9},... | collective-permute-start | bytes 196616 | tf_op jit(solution)/shard_map/ppermute | solution.py:79
  117.2 5.4 %collective-permute-start.18 = (f32[128,128]{1,0:T(8,128)S(1)}, f32[128,128]{1,0:T(8,128)S(1)}, u32[]{:S(2)}, u32[]{:S(2)}) collective-permute-start(f32[128,128]{1,0:T(8,128)S(1)} %get-tuple-element.3), channel_id=1, source_target_pairs={{0,8},{2,10},{4,12},{6,14},{8,0},{10,2},{12,4},{14,6},{1,9},{3,11}... | collective-permute-start | bytes 196616 | tf_op jit(solution)/shard_map/ppermute | solution.py:79
  122.6 4.3 %collective-permute-start.21 = (f32[128,128]{1,0:T(8,128)S(1)}, f32[128,128]{1,0:T(8,128)S(1)}, u32[]{:S(2)}, u32[]{:S(2)}) collective-permute-start(f32[128,128]{1,0:T(8,128)S(1)} %get-tuple-element.3), channel_id=1, source_target_pairs={{0,14},{2,0},{4,2},{6,4},{8,6},{10,8},{12,10},{14,12},{1,15},{3,1}... | collective-permute-start | bytes 196616 | tf_op jit(solution)/shard_map/ppermute | solution.py:79
  133.2 5.1 %copy-start.4 = (f32[1024]{0:T(1024)S(1)}, f32[1024]{0:T(1024)}, u32[]{:S(2)}) copy-start(f32[1024]{0:T(1024)} %get-tuple-element.28) | copy-start | bytes 12292
  133.2 5.1 %copy-start.5 = (f32[1024]{0:T(1024)S(1)}, f32[1024]{0:T(1024)}, u32[]{:S(2)}) copy-start(f32[1024]{0:T(1024)} %get-tuple-element.29) | copy-start | bytes 12292
  134.3 5.4 %copy-start.3 = (f32[1024]{0:T(1024)S(1)}, f32[1024]{0:T(1024)}, u32[]{:S(2)}) copy-start(f32[1024]{0:T(1024)} %get-tuple-element.27) | copy-start | bytes 12292
  138.0 8.9 %collective-permute-start.9 = (bf16[128,1024]{0,1:T(8,128)(2,1)}, bf16[128,1024]{0,1:T(8,128)(2,1)S(1)}, u32[]{:S(2)}, u32[]{:S(2)}) collective-permute-start(bf16[128,1024]{0,1:T(8,128)(2,1)} %collective-permute-done.7), channel_id=1, source_target_pairs={{4,8},{8,12},{12,14},{14,10},{10,6},{6,2},{2,0},{0,4},{5,9},{9,13}... | collective-permute-start | bytes 786440 | tf_op jit(solution)/shard_map/ppermute | solution.py:140
  141.3 7.7 %collective-permute-start.10 = (bf16[128,1024]{0,1:T(8,128)(2,1)}, bf16[128,1024]{0,1:T(8,128)(2,1)S(1)}, u32[]{:S(2)}, u32[]{:S(2)}) collective-permute-start(bf16[128,1024]{0,1:T(8,128)(2,1)} %collective-permute-done.8), channel_id=1, source_target_pairs={{8,4},{12,8},{14,12},{10,14},{6,10},{2,6},{0,2},{4,0},{9,5},{13,9}... | collective-permute-start | bytes 786440 | tf_op jit(solution)/shard_map/ppermute | solution.py:143
  146.9 9.2 %collective-permute-start.11 = (bf16[128,1024]{0,1:T(8,128)(2,1)S(1)}, bf16[128,1024]{0,1:T(8,128)(2,1)S(1)}, u32[]{:S(2)}, u32[]{:S(2)}) collective-permute-start(bf16[128,1024]{0,1:T(8,128)(2,1)S(1)} %collective-permute-done.9), channel_id=1, source_target_pairs={{4,8},{8,12},{12,14},{14,10},{10,6},{6,2},{2,0},{0,4},{5,9},{9,13}... | collective-permute-start | bytes 786440 | tf_op jit(solution)/shard_map/ppermute | solution.py:140
  149.0 0.7 copy-start.7
  150.4 6.8 %collective-permute-start.12 = (bf16[128,1024]{0,1:T(8,128)(2,1)}, bf16[128,1024]{0,1:T(8,128)(2,1)S(1)}, u32[]{:S(2)}, u32[]{:S(2)}) collective-permute-start(bf16[128,1024]{0,1:T(8,128)(2,1)} %copy-done.7), channel_id=1, source_target_pairs={{8,4},{12,8},{14,12},{10,14},{6,10},{2,6},{0,2},{4,0},{9,5},{13,9}... | collective-permute-start | bytes 786440 | tf_op jit(solution)/shard_map/ppermute | solution.py:143
  156.1 6.4 %collective-permute-start.13 = (bf16[128,1024]{0,1:T(8,128)(2,1)S(1)}, bf16[128,1024]{0,1:T(8,128)(2,1)S(1)}, u32[]{:S(2)}, u32[]{:S(2)}) collective-permute-start(bf16[128,1024]{0,1:T(8,128)(2,1)S(1)} %collective-permute-done.11), channel_id=1, source_target_pairs={{4,8},{8,12},{12,14},{14,10},{10,6},{6,2},{2,0},{0,4},{5,9},{9,13}... | collective-permute-start | bytes 786440 | tf_op jit(solution)/shard_map/ppermute | solution.py:140
where the time goes:
time: 165 us; the launch traced here: 164 us
  waiting for transfers between devices  49.3 us (30%)
  local copies, waits for them, and re-layouts  30.2 us (18%)
  other arithmetic  27.9 us (17%)
  starting transfers between devices  27.7 us (17%)
  matrix products  16.9 us (10%)
  between operations  11.7 us (7%)
    ppermute x14, waiting for transfers between devices, gather_blocks(): received.append(lax.ppermute(block, axis, pairs))  29 us
    ppermute x14, starting transfers between devices, gather_blocks(): received.append(lax.ppermute(block, axis, pairs))  16.8 us
    another operation x3, other arithmetic, invert(): factor = jnp.linalg.cholesky(matrix)  12.4 us
    another operation x2, other arithmetic, invert(): lax.linalg.triangular_solve(factor, identity, left_side=True, lower=True)  10.5 us
    all_to_all x1, waiting for transfers between devices, per_device(): expression_genes = lax.all_to_all(sent, 'cell', 1, 0, tiled=True)  9.38 us
    unnamed x32, local copies, waits for them, and re-layouts  8.62 us
    dot_general x26, matrix products, matmul(): return jnp.dot(left, right, precision=lax.Precision.HIGHEST)  8.15 us
    ppermute x4, waiting for transfers between devices, per_device(): ahead = lax.ppermute(ahead, 'cell', forward)  7.9 us
  transfers between devices with their start and end apart: 23, of which 15 were waited for; matrix products, arithmetic and copies ran while one was open for 36% of the time, Pallas kernels for 0%

commit v1 on v0

--- a/solution.py
+++ b/solution.py
@@ -100,7 +100,10 @@
     identity = jnp.eye(width, dtype=jnp.float32)
     design_all = gather_blocks(design, "cell").reshape(-1, width)
     sent = expression + (design_all[0, 0] * 0).astype(expression.dtype)
-    expression_genes = lax.all_to_all(sent, "cell", 1, 0, tiled=True)
+    expression_genes = jnp.concatenate(
+        lax.all_to_all(jnp.stack(jnp.split(sent, lax.axis_size("cell"), axis=1)), "cell", 0, 0),
+        axis=0,
+    )
     gram_total = lax.dot_general(
         design_all, design_all, (((0,), (0,)), ((), ())), preferred_element_type=jnp.float32
     )

time: 165 us -> 144 us (0.87)
  waiting for transfers between devices: 49.3 us -> 22.9 us
  starting transfers between devices: 27.7 us -> 33.2 us
  matrix products: 16.9 us -> 19.9 us
  other arithmetic: 27.9 us -> 26 us
    ppermute x14, waiting for transfers between devices: 29 us -> 11.3 us  [gather_blocks(): received.append(lax.ppermute(block, axis, pairs))]
    unnamed x32 -> x60, local copies, waits for them, and re-layouts: 8.62 us -> 20.7 us
    all_to_all x2 -> x0, local copies, waits for them, and re-layouts: 7.81 us -> none  [per_device(): expression_genes = lax.all_to_all(sent, 'cell', 1, 0, tiled=True)]
    all_to_all x1, waiting for transfers between devices: 9.38 us -> 1.64 us  [per_device(): lax.all_to_all(jnp.stack(jnp.split(sent, lax.axis_size('cell'), axis=1)),...]
    dynamic_update_slice x8, local copies, waits for them, and re-layouts: 5.77 us -> 0.19 us  [place(): return lax.dynamic_update_slice_in_dim(out, piece, start, axis=1)]
    ppermute x14, starting transfers between devices: 16.8 us -> 20.5 us  [gather_blocks(): received.append(lax.ppermute(block, axis, pairs))]
    dot_general x8, matrix products: 4.78 us -> 7.74 us  [place(): fitted = jnp.dot(design, block, preferred_element_type=jnp.float32)]
    ppermute x4, starting transfers between devices: 1.28 us -> 3.62 us  [per_device(): ahead = lax.ppermute(ahead, 'cell', forward)]
  transfers between devices with their start and end apart: 23 -> 23, of which waited for: 15 -> 13; matrix products, arithmetic and copies ran while one was open for 36% -> 41% of each run, Pallas kernels for 0% -> 0%
where the time goes in v1:
time: 144 us; the launch traced here: 143 us
  starting transfers between devices  33.2 us (23%)
  local copies, waits for them, and re-layouts  29.3 us (20%)
  other arithmetic  26 us (18%)
  waiting for transfers between devices  22.9 us (16%)
  matrix products  19.9 us (14%)
  between operations  11.5 us (8%)
    unnamed x60, local copies, waits for them, and re-layouts  20.7 us
    ppermute x14, starting transfers between devices, gather_blocks(): received.append(lax.ppermute(block, axis, pairs))  20.5 us
    another operation x3, other arithmetic, invert(): factor = jnp.linalg.cholesky(matrix)  12.4 us
    ppermute x14, waiting for transfers between devices, gather_blocks(): received.append(lax.ppermute(block, axis, pairs))  11.3 us
    another operation x2, other arithmetic, invert(): lax.linalg.triangular_solve(factor, identity, left_side=True, lower=True)  10.5 us
    dot_general x26, matrix products, matmul(): return jnp.dot(left, right, precision=lax.Precision.HIGHEST)  8.15 us
    dot_general x8, matrix products, place(): fitted = jnp.dot(design, block, preferred_element_type=jnp.float32)  7.74 us
    ppermute x4, waiting for transfers between devices, per_device(): ahead = lax.ppermute(ahead, 'cell', forward)  7.18 us
  transfers between devices with their start and end apart: 23, of which 13 were waited for; matrix products, arithmetic and copies ran while one was open for 41% of the time, Pallas kernels for 0%

profile of v1, /device:TPU:0, one launch (start us, length us, event | category | flops | bytes accessed | tf_op | source)
XLA Modules:
  0.0 142.9 jit_solution(13843700617807546983)
XLA Ops:
  0.6 3.0 %collective-permute-start = (bf16[128,128]{1,0:T(8,128)(2,1)}, bf16[128,128]{1,0:T(8,128)(2,1)S(1)}, u32[]{:S(2)}, u32[]{:S(2)}) collective-permute-start(bf16[128,128]{1,0:T(8,128)(2,1)} %param.6), channel_id=1, source_target_pairs={{0,2},{2,4},{4,6},{6,8},{8,10},{10,12},{12,14},{14,0},{1,3},{3,5},... | collective-permute-start | bytes 98312 | tf_op jit(solution)/shard_map/ppermute | solution.py:79
  3.6 1.6 %collective-permute-start.1 = (bf16[128,128]{1,0:T(8,128)(2,1)}, bf16[128,128]{1,0:T(8,128)(2,1)S(1)}, u32[]{:S(2)}, u32[]{:S(2)}) collective-permute-start(bf16[128,128]{1,0:T(8,128)(2,1)} %param.6), channel_id=1, source_target_pairs={{0,4},{2,6},{4,8},{6,10},{8,12},{10,14},{12,0},{14,2},{1,5},{3,7},... | collective-permute-start | bytes 98312 | tf_op jit(solution)/shard_map/ppermute | solution.py:79
  5.2 2.6 %collective-permute-start.2 = (bf16[128,128]{1,0:T(8,128)(2,1)}, bf16[128,128]{1,0:T(8,128)(2,1)S(1)}, u32[]{:S(2)}, u32[]{:S(2)}) collective-permute-start(bf16[128,128]{1,0:T(8,128)(2,1)} %param.6), channel_id=1, source_target_pairs={{0,6},{2,8},{4,10},{6,12},{8,14},{10,0},{12,2},{14,4},{1,7},{3,9},... | collective-permute-start | bytes 98312 | tf_op jit(solution)/shard_map/ppermute | solution.py:79
  7.8 1.2 collective-permute-start.3
  9.0 2.6 %collective-permute-start.4 = (bf16[128,128]{1,0:T(8,128)(2,1)}, bf16[128,128]{1,0:T(8,128)(2,1)S(1)}, u32[]{:S(2)}, u32[]{:S(2)}) collective-permute-start(bf16[128,128]{1,0:T(8,128)(2,1)} %param.6), channel_id=1, source_target_pairs={{0,10},{2,12},{4,14},{6,0},{8,2},{10,4},{12,6},{14,8},{1,11},{3,13... | collective-permute-start | bytes 98312 | tf_op jit(solution)/shard_map/ppermute | solution.py:79
  11.6 0.8 constant_dynamic-update-slice_fusion.7
  13.1 1.3 collective-permute-start.5
  14.4 1.5 %collective-permute-start.6 = (bf16[128,128]{1,0:T(8,128)(2,1)}, bf16[128,128]{1,0:T(8,128)(2,1)S(1)}, u32[]{:S(2)}, u32[]{:S(2)}) collective-permute-start(bf16[128,128]{1,0:T(8,128)(2,1)} %param.6), channel_id=1, source_target_pairs={{0,14},{2,0},{4,2},{6,4},{8,6},{10,8},{12,10},{14,12},{1,15},{3,1}... | collective-permute-start | bytes 98312 | tf_op jit(solution)/shard_map/ppermute | solution.py:79
  16.0 1.2 collective-permute-done.5
  17.2 1.4 collective-permute-done.6
  21.1 1.7 %broadcast_add_fusion = bf16[128,8192]{1,0:T(8,128)(2,1)S(1)} fusion(bf16[128,8192]{1,0:T(8,128)(2,1)} %param.5, bf16[]{:T(256)} %bitcast.11), kind=kLoop, calls=%fused_computation.38 | loop fusion | flops 1048576 | bytes 4194306 | tf_op jit(solution)/shard_map/add | solution.py:102
  22.8 0.7 fusion.24
  23.6 0.7 fusion.23
  24.3 0.7 fusion.22
  25.0 0.7 fusion.21
  25.7 0.7 fusion.20
  26.4 0.7 fusion.19
  27.2 0.7 fusion.18
  27.9 0.7 fusion.17
  28.6 5.5 %all-to-all-start = ((bf16[8,128,1024]{2,1,0:T(8,128)(2,1)}), bf16[8,128,1024]{2,1,0:T(8,128)(2,1)}, u32[]{:S(2)}, u32[]{:S(2)}) async-start(bf16[8,128,1024]{2,1,0:T(8,128)(2,1)} %fusion.17), calls=%async_computation | async-start | bytes 4194304 | tf_op jit(solution)/shard_map/all_to_all | solution.py:104
  44.3 1.0 constant_dynamic-slice_fusion
  45.3 1.9 %copy.30 = bf16[128,1024]{0,1:T(8,128)(2,1)} copy(bf16[128,1024]{1,0:T(8,128)(2,1)} %get-tuple-element.23) | data formatting | bytes 524288
  47.2 1.8 %copy.29 = bf16[128,1024]{0,1:T(8,128)(2,1)} copy(bf16[128,1024]{1,0:T(8,128)(2,1)} %get-tuple-element.24) | data formatting | bytes 524288
  49.0 1.8 %copy.28 = bf16[128,1024]{0,1:T(8,128)(2,1)} copy(bf16[128,1024]{1,0:T(8,128)(2,1)} %get-tuple-element.25) | data formatting | bytes 524288
  50.8 0.8 copy.27
  51.8 0.8 copy.31
  52.6 0.8 copy.32
  53.5 0.9 copy.33
  54.8 11.7 %cholesky.29 = f32[128,128]{1,0:T(8,128)S(1)} custom-call(f32[128,128]{1,0:T(8,128)S(1)} %fusion.30), custom_call_target="Cholesky" | custom-call | tf_op jit(solution)/shard_map/jit(cholesky)/cholesky | solution.py:18
  67.9 9.8 %custom-call.6 = f32[1,128,128]{1,2,0:T(8,128)S(1)} custom-call(f32[1,128,128]{2,1,0:T(8,128)S(1)} %fusion.26), custom_call_target="InvertDiagBlocksLowerTriangular" | custom-call | tf_op jit(solution)/shard_map/triangular_solve | solution.py:19
  78.2 1.6 %all-to-all-done = bf16[8,128,1024]{2,1,0:T(8,128)(2,1)} async-done(((bf16[8,128,1024]{2,1,0:T(8,128)(2,1)}), bf16[8,128,1024]{2,1,0:T(8,128)(2,1)}, u32[]{:S(2)}, u32[]{:S(2)}) %all-to-all-start) | async-done | bytes 2097184 | tf_op jit(solution)/shard_map/all_to_all | solution.py:104
  79.9 2.4 %convolution_bitcast_fusion.8 = f32[1024,128]{1,0:T(8,128)S(1)} fusion(bf16[8,128,1024]{2,1,0:T(8,128)(2,1)} %all-to-all-done, bf16[8,128,128]{2,1,0:T(8,128)(2,1)S(1)} %copy-done.3, pred[8]{0:T(512)(128)(4,1)S(1)} %compare_and_fusion), kind=kOutput, calls=%fused_computation.18 | convolution fusion | flops 268566528 | bytes 2883592 | tf_op jit(solution)/shard_map/dot_general | solution.py:111
  82.9 1.0 fusion.41
  83.9 1.3 collective-permute-start.8
  85.2 0.8 collective-permute-start.7
  86.5 0.7 collective-permute-done.14
  87.9 1.2 collective-permute-start.15
  90.0 2.4 %collective-permute-start.17 = (f32[128,128]{1,0:T(8,128)S(1)}, f32[128,128]{1,0:T(8,128)S(1)}, u32[]{:S(2)}, u32[]{:S(2)}) collective-permute-start(f32[128,128]{1,0:T(8,128)S(1)} %get-tuple-element.3), channel_id=1, source_target_pairs={{0,6},{2,8},{4,10},{6,12},{8,14},{10,0},{12,2},{14,4},{1,7},{3,9},... | collective-permute-start | bytes 196616 | tf_op jit(solution)/shard_map/ppermute | solution.py:79
  92.4 3.9 %collective-permute-done.15 = f32[128,128]{1,0:T(8,128)S(1)} collective-permute-done((f32[128,128]{1,0:T(8,128)S(1)}, f32[128,128]{1,0:T(8,128)S(1)}, u32[]{:S(2)}, u32[]{:S(2)}) %collective-permute-start.15) | collective-permute-done | bytes 65568 | tf_op jit(solution)/shard_map/ppermute | solution.py:79
  97.5 3.7 %collective-permute-done.17 = f32[128,128]{1,0:T(8,128)S(1)} collective-permute-done((f32[128,128]{1,0:T(8,128)S(1)}, f32[128,128]{1,0:T(8,128)S(1)}, u32[]{:S(2)}, u32[]{:S(2)}) %collective-permute-start.17) | collective-permute-done | bytes 65568 | tf_op jit(solution)/shard_map/ppermute | solution.py:79
  101.3 1.1 collective-permute-start.20
  103.0 1.2 collective-permute-start.21
  106.4 0.9 collective-permute-done.21
  107.9 1.6 %gather_fusion.1 = f32[8,128,128]{2,1,0:T(8,128)S(1)} fusion(f32[8,128,128]{2,1,0:T(8,128)} %bitcast_dynamic-update-slice_fusion, s32[1024]{0:T(1024)S(1)} %pad_clamp_fusion), kind=kCustom, calls=%fused_computation.1 | custom fusion | bytes 1048608 | tf_op jit(solution)/shard_map/jit(_take)/gather | solution.py:81
  110.3 0.8 fusion.16
  111.1 0.8 fusion.32
  116.4 1.4 fusion.8
  117.8 0.9 collective-permute-start.9
  118.7 1.3 subtract_convert_fusion.6
  120.1 1.3 subtract_convert_fusion.5
  121.7 1.2 collective-permute-start.10
  123.0 1.9 %collective-permute-done.9 = bf16[128,1024]{0,1:T(8,128)(2,1)} collective-permute-done((bf16[128,1024]{0,1:T(8,128)(2,1)}, bf16[128,1024]{0,1:T(8,128)(2,1)}, u32[]{:S(2)}, u32[]{:S(2)}) %collective-permute-start.9) | collective-permute-done | bytes 262176 | tf_op jit(solution)/shard_map/ppermute | solution.py:143
  124.9 1.1 collective-permute-start.11
  126.0 1.3 subtract_convert_fusion.4
  127.3 1.1 collective-permute-done.10
  128.4 0.7 copy-done.14
  129.7 1.2 collective-permute-start.12
  131.0 2.3 %collective-permute-done.11 = bf16[128,1024]{0,1:T(8,128)(2,1)} collective-permute-done((bf16[128,1024]{0,1:T(8,128)(2,1)}, bf16[128,1024]{0,1:T(8,128)(2,1)}, u32[]{:S(2)}, u32[]{:S(2)}) %collective-permute-start.11) | collective-permute-done | bytes 262176 | tf_op jit(solution)/shard_map/ppermute | solution.py:143
  133.3 0.8 collective-permute-start.13
  134.1 1.3 subtract_convert_fusion.2
  135.4 0.9 collective-permute-done.12
  137.1 3.0 %collective-permute-done.13 = bf16[128,1024]{0,1:T(8,128)(2,1)} collective-permute-done((bf16[128,1024]{0,1:T(8,128)(2,1)}, bf16[128,1024]{0,1:T(8,128)(2,1)}, u32[]{:S(2)}, u32[]{:S(2)}) %collective-permute-start.13) | collective-permute-done | bytes 262176 | tf_op jit(solution)/shard_map/ppermute | solution.py:143
  140.1 1.3 subtract_convert_fusion
  141.6 1.3 copy-done.1
  (124 shorter events, 19.9 us)
Async XLA Ops:
  0.6 12.4 %collective-permute-start = (bf16[128,128]{1,0:T(8,128)(2,1)}, bf16[128,128]{1,0:T(8,128)(2,1)S(1)}, u32[]{:S(2)}, u32[]{:S(2)}) collective-permute-start(bf16[128,128]{1,0:T(8,128)(2,1)} %param.6), channel_id=1, source_target_pairs={{0,2},{2,4},{4,6},{6,8},{8,10},{10,12},{12,14},{14,0},{1,3},{3,5},... | collective-permute-start | bytes 98312 | tf_op jit(solution)/shard_map/ppermute | solution.py:79
  3.6 10.8 %collective-permute-start.1 = (bf16[128,128]{1,0:T(8,128)(2,1)}, bf16[128,128]{1,0:T(8,128)(2,1)S(1)}, u32[]{:S(2)}, u32[]{:S(2)}) collective-permute-start(bf16[128,128]{1,0:T(8,128)(2,1)} %param.6), channel_id=1, source_target_pairs={{0,4},{2,6},{4,8},{6,10},{8,12},{10,14},{12,0},{14,2},{1,5},{3,7},... | collective-permute-start | bytes 98312 | tf_op jit(solution)/shard_map/ppermute | solution.py:79
  5.2 10.7 %collective-permute-start.2 = (bf16[128,128]{1,0:T(8,128)(2,1)}, bf16[128,128]{1,0:T(8,128)(2,1)S(1)}, u32[]{:S(2)}, u32[]{:S(2)}) collective-permute-start(bf16[128,128]{1,0:T(8,128)(2,1)} %param.6), channel_id=1, source_target_pairs={{0,6},{2,8},{4,10},{6,12},{8,14},{10,0},{12,2},{14,4},{1,7},{3,9},... | collective-permute-start | bytes 98312 | tf_op jit(solution)/shard_map/ppermute | solution.py:79
  7.8 8.2 %collective-permute-start.3 = (bf16[128,128]{1,0:T(8,128)(2,1)}, bf16[128,128]{1,0:T(8,128)(2,1)S(1)}, u32[]{:S(2)}, u32[]{:S(2)}) collective-permute-start(bf16[128,128]{1,0:T(8,128)(2,1)} %param.6), channel_id=1, source_target_pairs={{0,8},{2,10},{4,12},{6,14},{8,0},{10,2},{12,4},{14,6},{1,9},{3,11}... | collective-permute-start | bytes 98312 | tf_op jit(solution)/shard_map/ppermute | solution.py:79
  9.0 6.9 %collective-permute-start.4 = (bf16[128,128]{1,0:T(8,128)(2,1)}, bf16[128,128]{1,0:T(8,128)(2,1)S(1)}, u32[]{:S(2)}, u32[]{:S(2)}) collective-permute-start(bf16[128,128]{1,0:T(8,128)(2,1)} %param.6), channel_id=1, source_target_pairs={{0,10},{2,12},{4,14},{6,0},{8,2},{10,4},{12,6},{14,8},{1,11},{3,13... | collective-permute-start | bytes 98312 | tf_op jit(solution)/shard_map/ppermute | solution.py:79
  13.1 4.1 %collective-permute-start.5 = (bf16[128,128]{1,0:T(8,128)(2,1)}, bf16[128,128]{1,0:T(8,128)(2,1)S(1)}, u32[]{:S(2)}, u32[]{:S(2)}) collective-permute-start(bf16[128,128]{1,0:T(8,128)(2,1)} %param.6), channel_id=1, source_target_pairs={{0,12},{2,14},{4,0},{6,2},{8,4},{10,6},{12,8},{14,10},{1,13},{3,15... | collective-permute-start | bytes 98312 | tf_op jit(solution)/shard_map/ppermute | solution.py:79
  14.4 4.2 %collective-permute-start.6 = (bf16[128,128]{1,0:T(8,128)(2,1)}, bf16[128,128]{1,0:T(8,128)(2,1)S(1)}, u32[]{:S(2)}, u32[]{:S(2)}) collective-permute-start(bf16[128,128]{1,0:T(8,128)(2,1)} %param.6), channel_id=1, source_target_pairs={{0,14},{2,0},{4,2},{6,4},{8,6},{10,8},{12,10},{14,12},{1,15},{3,1}... | collective-permute-start | bytes 98312 | tf_op jit(solution)/shard_map/ppermute | solution.py:79
  19.2 3.6 %copy-start.2 = (bf16[8,128,128]{2,1,0:T(8,128)(2,1)}, bf16[8,128,128]{2,1,0:T(8,128)(2,1)S(1)}, u32[]{:S(2)}) copy-start(bf16[8,128,128]{2,1,0:T(8,128)(2,1)S(1)} %gather_fusion) | copy-start | bytes 786436
  28.6 5.5 %copy-start.15 = (s32[8]{0:T(128)S(1)}, s32[8]{0:T(128)}, u32[]{:S(2)}) copy-start(s32[8]{0:T(128)} %constant.188.clone) | copy-start | bytes 100
  28.6 10.8 %copy-start.13 = (s32[8]{0:T(128)S(1)}, s32[8]{0:T(128)}, u32[]{:S(2)}) copy-start(s32[8]{0:T(128)} %constant.187.clone) | copy-start | bytes 100
  28.6 15.7 %copy-start = (bf16[128,8192]{1,0:T(8,128)(2,1)S(1)}, bf16[128,8192]{1,0:T(8,128)(2,1)}, u32[]{:S(2)}) copy-start(bf16[128,8192]{1,0:T(8,128)(2,1)} %param.5) | copy-start | bytes 6291460
  28.6 51.3 %all-to-all-start = ((bf16[8,128,1024]{2,1,0:T(8,128)(2,1)}), bf16[8,128,1024]{2,1,0:T(8,128)(2,1)}, u32[]{:S(2)}, u32[]{:S(2)}) async-start(bf16[8,128,1024]{2,1,0:T(8,128)(2,1)} %fusion.17), calls=%async_computation | async-start | bytes 4194304 | tf_op jit(solution)/shard_map/all_to_all | solution.py:104
  45.3 9.0 %copy-start.12 = (f32[8192]{0:T(1024)S(1)}, f32[8192]{0:T(1024)}, u32[]{:S(2)}) copy-start(f32[8192]{0:T(1024)} %param.7) | copy-start | bytes 98308
  45.3 9.0 %copy-start.3 = (bf16[8,128,128]{2,1,0:T(8,128)(2,1)S(1)}, bf16[8,128,128]{2,1,0:T(8,128)(2,1)}, u32[]{:S(2)}) copy-start(bf16[8,128,128]{2,1,0:T(8,128)(2,1)} %copy-done.2) | copy-start | bytes 786436
  82.3 3.7 %copy-start.11 = (bf16[128,128]{1,0:T(8,128)(2,1)S(1)}, bf16[128,128]{1,0:T(8,128)(2,1)}, u32[]{:S(2)}) copy-start(bf16[128,128]{1,0:T(8,128)(2,1)} %param.6) | copy-start | bytes 98308
  83.9 36.1 %collective-permute-start.8 = (bf16[128,1024]{0,1:T(8,128)(2,1)S(1)}, bf16[128,1024]{0,1:T(8,128)(2,1)}, u32[]{:S(2)}, u32[]{:S(2)}) collective-permute-start(bf16[128,1024]{0,1:T(8,128)(2,1)S(1)} %convert_bitcast_fusion), channel_id=1, source_target_pairs={{8,4},{12,8},{14,12},{10,14},{6,10},{2,6},{0,2},{4,0},{9,5},{13,9}... | collective-permute-start | bytes 786440 | tf_op jit(solution)/shard_map/ppermute | solution.py:146
  85.2 32.6 %collective-permute-start.7 = (bf16[128,1024]{0,1:T(8,128)(2,1)S(1)}, bf16[128,1024]{0,1:T(8,128)(2,1)}, u32[]{:S(2)}, u32[]{:S(2)}) collective-permute-start(bf16[128,1024]{0,1:T(8,128)(2,1)S(1)} %convert_bitcast_fusion), channel_id=1, source_target_pairs={{4,8},{8,12},{12,14},{14,10},{10,6},{6,2},{2,0},{0,4},{5,9},{9,13}... | collective-permute-start | bytes 786440 | tf_op jit(solution)/shard_map/ppermute | solution.py:143
  86.0 1.3 collective-permute-start.14
  87.9 8.4 %collective-permute-start.15 = (f32[128,128]{1,0:T(8,128)S(1)}, f32[128,128]{1,0:T(8,128)S(1)}, u32[]{:S(2)}, u32[]{:S(2)}) collective-permute-start(f32[128,128]{1,0:T(8,128)S(1)} %get-tuple-element.3), channel_id=1, source_target_pairs={{0,2},{2,4},{4,6},{6,8},{8,10},{10,12},{12,14},{14,0},{1,3},{3,5},... | collective-permute-start | bytes 196616 | tf_op jit(solution)/shard_map/ppermute | solution.py:79
  89.4 7.5 %collective-permute-start.16 = (f32[128,128]{1,0:T(8,128)S(1)}, f32[128,128]{1,0:T(8,128)S(1)}, u32[]{:S(2)}, u32[]{:S(2)}) collective-permute-start(f32[128,128]{1,0:T(8,128)S(1)} %get-tuple-element.3), channel_id=1, source_target_pairs={{0,4},{2,6},{4,8},{6,10},{8,12},{10,14},{12,0},{14,2},{1,5},{3,7},... | collective-permute-start | bytes 196616 | tf_op jit(solution)/shard_map/ppermute | solution.py:79
  90.0 11.2 %collective-permute-start.17 = (f32[128,128]{1,0:T(8,128)S(1)}, f32[128,128]{1,0:T(8,128)S(1)}, u32[]{:S(2)}, u32[]{:S(2)}) collective-permute-start(f32[128,128]{1,0:T(8,128)S(1)} %get-tuple-element.3), channel_id=1, source_target_pairs={{0,6},{2,8},{4,10},{6,12},{8,14},{10,0},{12,2},{14,4},{1,7},{3,9},... | collective-permute-start | bytes 196616 | tf_op jit(solution)/shard_map/ppermute | solution.py:79
  96.3 6.7 %collective-permute-start.18 = (f32[128,128]{1,0:T(8,128)S(1)}, f32[128,128]{1,0:T(8,128)S(1)}, u32[]{:S(2)}, u32[]{:S(2)}) collective-permute-start(f32[128,128]{1,0:T(8,128)S(1)} %get-tuple-element.3), channel_id=1, source_target_pairs={{0,8},{2,10},{4,12},{6,14},{8,0},{10,2},{12,4},{14,6},{1,9},{3,11}... | collective-permute-start | bytes 196616 | tf_op jit(solution)/shard_map/ppermute | solution.py:79
  96.9 8.0 %collective-permute-start.19 = (f32[128,128]{1,0:T(8,128)S(1)}, f32[128,128]{1,0:T(8,128)S(1)}, u32[]{:S(2)}, u32[]{:S(2)}) collective-permute-start(f32[128,128]{1,0:T(8,128)S(1)} %get-tuple-element.3), channel_id=1, source_target_pairs={{0,10},{2,12},{4,14},{6,0},{8,2},{10,4},{12,6},{14,8},{1,11},{3,13... | collective-permute-start | bytes 196616 | tf_op jit(solution)/shard_map/ppermute | solution.py:79
  101.3 4.5 %collective-permute-start.20 = (f32[128,128]{1,0:T(8,128)S(1)}, f32[128,128]{1,0:T(8,128)S(1)}, u32[]{:S(2)}, u32[]{:S(2)}) collective-permute-start(f32[128,128]{1,0:T(8,128)S(1)} %get-tuple-element.3), channel_id=1, source_target_pairs={{0,12},{2,14},{4,0},{6,2},{8,4},{10,6},{12,8},{14,10},{1,13},{3,15... | collective-permute-start | bytes 196616 | tf_op jit(solution)/shard_map/ppermute | solution.py:79
  103.0 4.3 %collective-permute-start.21 = (f32[128,128]{1,0:T(8,128)S(1)}, f32[128,128]{1,0:T(8,128)S(1)}, u32[]{:S(2)}, u32[]{:S(2)}) collective-permute-start(f32[128,128]{1,0:T(8,128)S(1)} %get-tuple-element.3), channel_id=1, source_target_pairs={{0,14},{2,0},{4,2},{6,4},{8,6},{10,8},{12,10},{14,12},{1,15},{3,1}... | collective-permute-start | bytes 196616 | tf_op jit(solution)/shard_map/ppermute | solution.py:79
  113.0 5.7 %copy-start.10 = (bf16[128,1024]{0,1:T(8,128)(2,1)S(1)}, bf16[128,1024]{0,1:T(8,128)(2,1)}, u32[]{:S(2)}) copy-start(bf16[128,1024]{0,1:T(8,128)(2,1)} %copy.27) | copy-start | bytes 786436
  114.1 6.0 %copy-start.9 = (bf16[128,1024]{0,1:T(8,128)(2,1)S(1)}, bf16[128,1024]{0,1:T(8,128)(2,1)}, u32[]{:S(2)}) copy-start(bf16[128,1024]{0,1:T(8,128)(2,1)} %copy.28) | copy-start | bytes 786436
  117.8 8.2 %copy-start.8 = (bf16[128,1024]{0,1:T(8,128)(2,1)S(1)}, bf16[128,1024]{0,1:T(8,128)(2,1)}, u32[]{:S(2)}) copy-start(bf16[128,1024]{0,1:T(8,128)(2,1)} %copy.29) | copy-start | bytes 786436
  117.8 7.1 %collective-permute-start.9 = (bf16[128,1024]{0,1:T(8,128)(2,1)}, bf16[128,1024]{0,1:T(8,128)(2,1)}, u32[]{:S(2)}, u32[]{:S(2)}) collective-permute-start(bf16[128,1024]{0,1:T(8,128)(2,1)} %collective-permute-done.7), channel_id=1, source_target_pairs={{4,8},{8,12},{12,14},{14,10},{10,6},{6,2},{2,0},{0,4},{5,9},{9,13}... | collective-permute-start | bytes 786440 | tf_op jit(solution)/shard_map/ppermute | solution.py:143
  120.0 9.0 %copy-start.7 = (bf16[128,1024]{0,1:T(8,128)(2,1)S(1)}, bf16[128,1024]{0,1:T(8,128)(2,1)}, u32[]{:S(2)}) copy-start(bf16[128,1024]{0,1:T(8,128)(2,1)} %copy.30) | copy-start | bytes 786436
  121.7 6.6 %collective-permute-start.10 = (bf16[128,1024]{0,1:T(8,128)(2,1)}, bf16[128,1024]{0,1:T(8,128)(2,1)S(1)}, u32[]{:S(2)}, u32[]{:S(2)}) collective-permute-start(bf16[128,1024]{0,1:T(8,128)(2,1)} %collective-permute-done.8), channel_id=1, source_target_pairs={{8,4},{12,8},{14,12},{10,14},{6,10},{2,6},{0,2},{4,0},{9,5},{13,9}... | collective-permute-start | bytes 786440 | tf_op jit(solution)/shard_map/ppermute | solution.py:146
  123.0 11.1 %copy-start.6 = (bf16[128,1024]{0,1:T(8,128)(2,1)S(1)}, bf16[128,1024]{0,1:T(8,128)(2,1)}, u32[]{:S(2)}) copy-start(bf16[128,1024]{0,1:T(8,128)(2,1)} %copy.31) | copy-start | bytes 786436
  124.9 8.4 %collective-permute-start.11 = (bf16[128,1024]{0,1:T(8,128)(2,1)}, bf16[128,1024]{0,1:T(8,128)(2,1)}, u32[]{:S(2)}, u32[]{:S(2)}) collective-permute-start(bf16[128,1024]{0,1:T(8,128)(2,1)} %collective-permute-done.9), channel_id=1, source_target_pairs={{4,8},{8,12},{12,14},{14,10},{10,6},{6,2},{2,0},{0,4},{5,9},{9,13}... | collective-permute-start | bytes 786440 | tf_op jit(solution)/shard_map/ppermute | solution.py:143
  127.3 9.1 %copy-start.5 = (bf16[128,1024]{0,1:T(8,128)(2,1)S(1)}, bf16[128,1024]{0,1:T(8,128)(2,1)}, u32[]{:S(2)}) copy-start(bf16[128,1024]{0,1:T(8,128)(2,1)} %copy.32) | copy-start | bytes 786436
  128.4 0.7 copy-start.14
  129.7 6.6 %collective-permute-start.12 = (bf16[128,1024]{0,1:T(8,128)(2,1)}, bf16[128,1024]{0,1:T(8,128)(2,1)S(1)}, u32[]{:S(2)}, u32[]{:S(2)}) collective-permute-start(bf16[128,1024]{0,1:T(8,128)(2,1)} %copy-done.14), channel_id=1, source_target_pairs={{8,4},{12,8},{14,12},{10,14},{6,10},{2,6},{0,2},{4,0},{9,5},{13,9}... | collective-permute-start | bytes 786440 | tf_op jit(solution)/shard_map/ppermute | solution.py:146
  131.0 9.1 %copy-start.4 = (bf16[128,1024]{0,1:T(8,128)(2,1)S(1)}, bf16[128,1024]{0,1:T(8,128)(2,1)}, u32[]{:S(2)}) copy-start(bf16[128,1024]{0,1:T(8,128)(2,1)} %copy.33) | copy-start | bytes 786436
  133.3 6.8 %collective-permute-start.13 = (bf16[128,1024]{0,1:T(8,128)(2,1)}, bf16[128,1024]{0,1:T(8,128)(2,1)}, u32[]{:S(2)}, u32[]{:S(2)}) collective-permute-start(bf16[128,1024]{0,1:T(8,128)(2,1)} %collective-permute-done.11), channel_id=1, source_target_pairs={{4,8},{8,12},{12,14},{14,10},{10,6},{6,2},{2,0},{0,4},{5,9},{9,13}... | collective-permute-start | bytes 786440 | tf_op jit(solution)/shard_map/ppermute | solution.py:143
  141.6 1.3 copy-start.1
